TPU v7x, 512 devices: a whole 4x4x16 slice. The times are simulated.
512 devices in a mesh: ctx: 32 (over z_hi, x, y), exp: 16 (over z_lo, core).
Axes of the slice: x: 4, y: 4, z: 16 (z_hi: 2, z_lo: 8; z = z_hi * 8 + z_lo), core: 2. Of those that a mesh axis runs over, the one named last changes fastest.
Arguments:
- residual: bfloat16 [4096, 4096], P(('ctx', 'exp')), may hold values from -6 to 6
- queries: bfloat16 [4096, 4096], P('ctx', 'exp'), may hold values from -8 to 8
- keys: bfloat16 [4096, 256], P('ctx'), may hold values from -8 to 8
- values: bfloat16 [4096, 256], P('ctx'), may hold values from -6 to 6
- span_pos: int32 [64], replicated, may hold values from 0 to 63, each once
- out_proj: bfloat16 [4096, 4096], P('exp'), may hold values from -0.71875 to 0.71875
- norm_gain: float32 [4096], replicated, may hold values from 0.25 to 1.75
- expert_gate: bfloat16 [16, 4096, 768], P('exp', None, 'ctx'), may hold values from -0.09375 to 0.09375
- expert_up: bfloat16 [16, 4096, 768], P('exp', None, 'ctx'), may hold values from -0.09375 to 0.09375
- expert_ids: int32 [4096, 8], P(('ctx', 'exp')), may hold values from 0 to 15, all different within a row; in each aligned block of 8 rows (0 to 7, 8 to 15, ...) at most 6 rows name the same one
- route_weight: float32 [4096, 8], P(('ctx', 'exp')), may hold values from 0.25 to 2
Outputs:
- mixed: bfloat16 [4096, 4096], P(('ctx', 'exp'))
- routed: bfloat16 [4096, 8, 768], P(('ctx', 'exp'))
Inputs may be any that keep to these rules, and one draw needn't show every extreme that they name: `span_pos`: every span number appears once. `expert_ids`: each row names 8 different experts; among the rows of one device (8 rows in a row, aligned) no expert is named more than 6 times, and in some device's rows some expert is named exactly 6 times.
All inputs are finite; a program needn't handle non-finite values.
Results may differ from a plain program's by a relative error of at most 0.035.
Values may be sent and summed in bfloat16 or wider, within the bound.
No kernel may reach another device: no remote copies, remote signals or barrier semaphores. Data moves between devices by JAX's collectives and lax.ppermute only.
A program may use at most 128 MiB of HBM per device.

v0:
```python
import math
import jax
import jax.numpy as jnp
import numpy as np
from jax import lax
from jax.sharding import Mesh
from jax.sharding import PartitionSpec as P

D = 4096
HQ = 32
KVH = 2
HD = 128
FE = 768
EXPERTS = 16
TOPK = 8
CH = 64
CTX = ("zh", "x", "y")
EXP = ("zl", "c")


def stored_positions(span_pos, rows):
    span = rows // CH
    table = span[:, None] == jnp.arange(span_pos.shape[0], dtype=jnp.int32)[None, :]
    base = jnp.sum(jnp.where(table, span_pos[None, :], 0), axis=1)
    return base * CH + rows % CH


def doubling_bits(n):
    bits = []
    b = n // 2
    while b >= 1:
        bits.append(b)
        b //= 2
    return bits


def gather_by_doubling(piece, n):
    idx = lax.axis_index(CTX)
    cur = piece
    order = [0]
    for bit in doubling_bits(n):
        other = lax.ppermute(cur, CTX, [(i, i ^ bit) for i in range(n)])
        low = idx & bit == 0
        cur = jnp.where(low, jnp.concatenate([cur, other]), jnp.concatenate([other, cur]))
        order = order + [o + bit for o in order]
    return (cur, order)


def shards(
    residual,
    queries,
    keys,
    values,
    span_pos,
    out_proj,
    norm_gain,
    expert_gate,
    expert_up,
    expert_ids,
    route_weight,
    n_ctx,
    n_xy,
    n_zh,
):
    tok_rows = queries.shape[0]
    per_device = queries.shape[1] // HD
    group = HQ // KVH
    ctx_index = lax.axis_index(CTX)
    exp_index = lax.axis_index(EXP)
    n_exp = EXPERTS
    fe_dev = expert_gate.shape[2]
    w_local = jnp.concatenate([expert_gate[0].T, expert_up[0].T], axis=0)
    zh_index = lax.axis_index("zh")
    core_index = lax.axis_index("c")
    kv_head = exp_index * per_device // group
    own_keys = lax.dynamic_slice_in_dim(keys, kv_head * HD, HD, 1)
    own_values = lax.dynamic_slice_in_dim(values, kv_head * HD, HD, 1)
    kv_local = jnp.where(core_index == 0, own_keys, own_values)
    bits = doubling_bits(n_ctx)
    first = bits[0]
    kv_other = lax.ppermute(kv_local, CTX, [(i, i ^ first) for i in range(n_ctx)])
    w_other = lax.ppermute(w_local, "zh", [(0, 1), (1, 0)])
    w_pair = jnp.where(
        zh_index == 0, jnp.concatenate([w_local, w_other]), jnp.concatenate([w_other, w_local])
    )
    w_all = lax.all_gather(w_pair, ("x", "y"), axis=0, tiled=True)
    low = ctx_index & first == 0
    cur = jnp.where(
        low, jnp.concatenate([kv_local, kv_other]), jnp.concatenate([kv_other, kv_local])
    )
    order = [0, first]
    for bit in bits[1:]:
        other = lax.ppermute(cur, CTX, [(i, i ^ bit) for i in range(n_ctx)])
        low = ctx_index & bit == 0
        cur = jnp.where(low, jnp.concatenate([cur, other]), jnp.concatenate([other, cur]))
        order = order + [o + bit for o in order]
    partner = lax.ppermute(cur, "c", [(0, 1), (1, 0)])
    key_piece = jnp.where(core_index == 0, cur, partner)
    value_piece = jnp.where(core_index == 0, partner, cur)
    length = key_piece.shape[0]
    block_ctx = jnp.asarray(np.array(order, np.int32))
    key_rows_all = jnp.repeat(block_ctx, tok_rows) * tok_rows + jnp.tile(
        jnp.arange(tok_rows, dtype=jnp.int32), n_ctx
    )
    query_pos = stored_positions(
        span_pos, ctx_index * tok_rows + jnp.arange(tok_rows, dtype=jnp.int32)
    )
    query_heads = queries.reshape(tok_rows, per_device, HD)
    scale = 1.0 / math.sqrt(HD)
    carry = (
        jnp.full((per_device, tok_rows), -1e30, jnp.float32),
        jnp.zeros((per_device, tok_rows), jnp.float32),
        jnp.zeros((per_device, tok_rows, HD), jnp.float32),
    )
    block = min(length, 1024)
    for begin in range(0, length, block):
        stop = min(begin + block, length)
        attend_key_piece = key_piece[begin:stop]
        attend_value_piece = value_piece[begin:stop]
        attend_running, attend_total, attend_accum = carry
        key_pos = stored_positions(span_pos, key_rows_all[begin:stop])
        scores = (
            jnp.einsum(
                "tqd,nd->qtn", query_heads, attend_key_piece, preferred_element_type=jnp.float32
            )
            * scale
        )
        visible = key_pos[None, None, :] <= query_pos[None, :, None]
        block_top = jnp.max(jnp.where(visible, scores, -1e30), axis=2)
        new_top = jnp.maximum(attend_running, block_top)
        factor = jnp.exp(attend_running - new_top)
        probs = jnp.where(visible, jnp.exp(scores - new_top[:, :, None]), 0.0)
        attend_total = attend_total * factor + jnp.sum(probs, axis=2)
        summed = jnp.einsum(
            "qtn,nd->qtd",
            probs.astype(jnp.bfloat16),
            attend_value_piece,
            preferred_element_type=jnp.float32,
        )
        attend_accum = attend_accum * factor[:, :, None] + summed
        carry = (new_top, attend_total, attend_accum)
    running, total, accum = carry
    attn = (accum / total[:, :, None]).astype(jnp.bfloat16)
    attn = jnp.transpose(attn, (1, 0, 2)).reshape(tok_rows, per_device * HD)
    tok_dev = residual.shape[0]
    share = jnp.dot(attn, out_proj, preferred_element_type=jnp.float32).astype(jnp.bfloat16)
    zl_index = lax.axis_index("zl")
    n_zl = n_exp // 2
    by_core = jnp.transpose(share.reshape(n_zl, 2, tok_dev, D), (1, 0, 2, 3))
    keep = jnp.where(core_index == 0, by_core[0], by_core[1])
    give = jnp.where(core_index == 0, by_core[1], by_core[0])
    got = lax.ppermute(give, "c", [(0, 1), (1, 0)])
    part = keep.astype(jnp.float32) + got.astype(jnp.float32)
    pair_sum = part.astype(jnp.bfloat16)
    shares = lax.all_to_all(pair_sum, "zl", split_axis=0, concat_axis=0, tiled=True)
    head_total = jnp.sum(shares.astype(jnp.float32), axis=0)
    mixed = (residual.astype(jnp.float32) + head_total).astype(jnp.bfloat16)
    mixed_f = mixed.astype(jnp.float32)
    square = jnp.mean(mixed_f * mixed_f, axis=1, keepdims=True)
    normed = (mixed_f * lax.rsqrt(square + 1e-06) * norm_gain[None, :]).astype(jnp.bfloat16)
    ids_rw = jnp.concatenate([expert_ids.astype(jnp.float32), route_weight], axis=1)
    ids_rw_all = lax.all_to_all(
        jnp.broadcast_to(ids_rw[None], (n_exp,) + ids_rw.shape),
        EXP,
        split_axis=0,
        concat_axis=0,
        tiled=True,
    ).reshape(n_exp * tok_dev, 2 * TOPK)
    ids_all = ids_rw_all[:, :TOPK].astype(jnp.int32)
    rw_all = ids_rw_all[:, TOPK:]
    cur = normed
    order = [0]
    for bit in doubling_bits(n_zl):
        other = lax.ppermute(cur, "zl", [(i, i ^ bit) for i in range(n_zl)])
        low = zl_index & bit == 0
        cur = jnp.where(low, jnp.concatenate([cur, other]), jnp.concatenate([other, cur]))
        order = order + [o + bit for o in order]
    partner = lax.ppermute(cur, "c", [(0, 1), (1, 0)])
    both = jnp.where(
        core_index == 0, jnp.concatenate([cur, partner]), jnp.concatenate([partner, cur])
    )
    blocks = []
    for src in range(n_exp):
        q = src % 2 * n_zl + order.index(src // 2)
        blocks.append(both[q * tok_dev : (q + 1) * tok_dev])
    gathered = jnp.concatenate(blocks)
    normed_all = gathered
    most_slots = tok_dev
    chosen = jnp.any(ids_all == exp_index, axis=1).astype(jnp.int32).reshape(n_exp, tok_dev)
    rank = jnp.cumsum(chosen, axis=1) - chosen
    dest = jnp.where(
        chosen == 1, jnp.arange(n_exp, dtype=jnp.int32)[:, None] * most_slots + rank, -1
    ).reshape(-1)
    slot_of = jnp.arange(n_exp * most_slots, dtype=jnp.int32)[:, None] == dest[None, :]
    placing = slot_of.astype(jnp.bfloat16)
    rw_tok = jnp.sum(jnp.where(ids_all == exp_index, rw_all, 0.0), axis=1)
    rw_slot = jnp.sum(jnp.where(slot_of, rw_tok[None, :], 0.0), axis=1)
    received = jnp.dot(placing, normed_all, preferred_element_type=jnp.float32).astype(jnp.bfloat16)
    received = lax.optimization_barrier(received)
    ids_flat = expert_ids.reshape(-1)
    onehot = (ids_flat[:, None] == jnp.arange(EXPERTS, dtype=jnp.int32)[None, :]).astype(jnp.int32)
    earlier = jnp.cumsum(onehot, axis=0) - onehot
    slot = jnp.sum(earlier * onehot, axis=1)
    target = ids_flat * most_slots + slot
    proj = jnp.einsum("fd,sd->fs", w_all, received, preferred_element_type=jnp.float32)
    proj = proj.reshape(n_xy, n_zh, 2, fe_dev, EXPERTS * most_slots)
    hidden = jax.nn.silu(proj[:, :, 0]) * proj[:, :, 1]
    hidden = jnp.transpose(hidden, (1, 0, 2, 3)).reshape(FE, EXPERTS * most_slots)
    hidden = (hidden * rw_slot[None, :]).astype(jnp.bfloat16).T.reshape(EXPERTS, most_slots, FE)
    returned = lax.all_to_all(hidden, EXP, split_axis=0, concat_axis=0, tiled=True).reshape(
        EXPERTS * most_slots, FE
    )
    routed = jnp.take(returned, target, axis=0)
    return (mixed, routed.reshape(tok_dev, TOPK, FE))


def solution(mesh):
    n_ctx = mesh.shape["ctx"]
    n_exp = mesh.shape["exp"]
    n_zh = 2
    n_xy = n_ctx // n_zh
    side = int(round(math.sqrt(n_xy)))
    n_zl = n_exp // 2
    fine = Mesh(mesh.devices.reshape(n_zh, side, n_xy // side, n_zl, 2), CTX + EXP)
    tok = CTX + EXP
    in_specs = (
        P(tok, None),
        P(CTX, EXP),
        P(CTX, None),
        P(CTX, None),
        P(),
        P(EXP, None),
        P(),
        P(EXP, None, CTX),
        P(EXP, None, CTX),
        P(tok, None),
        P(tok, None),
    )
    out_specs = (P(tok, None), P(tok, None, None))

    def body(*args):
        return shards(*args, n_ctx=n_ctx, n_xy=n_xy, n_zh=n_zh)

    return jax.shard_map(body, mesh=fine, in_specs=in_specs, out_specs=out_specs, check_vma=False)
```

profile of v0, /device:TPU:1, one launch (start us, length us, event | category | flops | bytes accessed | tf_op | source)
XLA Modules:
  0.0 239.2 jit_solution(13024758327320912529)
XLA Ops:
  8.2 16.3 %collective-permute-start = (bf16[128,128]{1,0:T(8,128)(2,1)S(1)}, bf16[128,128]{1,0:T(8,128)(2,1)S(1)}, u32[]{:S(2)}, u32[]{:S(2)}) collective-permute-start(bf16[128,128]{1,0:T(8,128)(2,1)S(1)} %dynamic-slice_select_fusion), channel_id=1, source_target_pairs={{0,256},{16,272},{32,288},{48,304},{64,320},{80,336},{96,352},{112... | collective-permute-start | bytes 98312 | tf_op jit(solution)/shard_map/ppermute | solution.py:81
  25.9 4.7 %collective-permute-start.1 = (bf16[256,128]{1,0:T(8,128)(2,1)S(1)}, bf16[256,128]{1,0:T(8,128)(2,1)S(1)}, u32[]{:S(2)}, u32[]{:S(2)}) collective-permute-start(bf16[256,128]{1,0:T(8,128)(2,1)S(1)} %maximum_select_fusion.9), channel_id=1, source_target_pairs={{0,128},{16,144},{32,160},{48,176},{64,192},{80,208},{96,224},{112... | collective-permute-start | bytes 196616 | tf_op jit(solution)/shard_map/ppermute | solution.py:93
  32.4 3.1 %collective-permute-start.2 = (bf16[512,128]{1,0:T(8,128)(2,1)S(1)}, bf16[512,128]{1,0:T(8,128)(2,1)S(1)}, u32[]{:S(2)}, u32[]{:S(2)}) collective-permute-start(bf16[512,128]{1,0:T(8,128)(2,1)S(1)} %maximum_select_fusion.7), channel_id=1, source_target_pairs={{0,64},{16,80},{32,96},{48,112},{64,0},{80,16},{96,32},{112,48},{1... | collective-permute-start | bytes 393224 | tf_op jit(solution)/shard_map/ppermute | solution.py:93
  35.6 2.6 %collective-permute-done.2 = bf16[512,128]{1,0:T(8,128)(2,1)S(1)} collective-permute-done((bf16[512,128]{1,0:T(8,128)(2,1)S(1)}, bf16[512,128]{1,0:T(8,128)(2,1)S(1)}, u32[]{:S(2)}, u32[]{:S(2)}) %collective-permute-start.2) | collective-permute-done | bytes 131104 | tf_op jit(solution)/shard_map/ppermute | solution.py:93
  38.2 4.8 %collective-permute-start.3 = (bf16[1024,128]{1,0:T(8,128)(2,1)S(1)}, bf16[1024,128]{1,0:T(8,128)(2,1)S(1)}, u32[]{:S(2)}, u32[]{:S(2)}) collective-permute-start(bf16[1024,128]{1,0:T(8,128)(2,1)S(1)} %maximum_select_fusion.5), channel_id=1, source_target_pairs={{0,32},{16,48},{32,0},{48,16},{64,96},{80,112},{96,64},{112,80},{1... | collective-permute-start | bytes 786440 | tf_op jit(solution)/shard_map/ppermute | solution.py:93
  44.9 12.5 %collective-permute-start.7 = (bf16[48,4096]{1,0:T(8,128)(2,1)}, bf16[48,4096]{1,0:T(8,128)(2,1)}, u32[]{:S(2)}, u32[]{:S(2)}) collective-permute-start(bf16[48,4096]{1,0:T(8,128)(2,1)} %pad_maximum_fusion), channel_id=1, source_target_pairs={{0,256},{256,0},{1,257},{257,1},{2,258},{258,2},{3,259},{259,3},{4... | collective-permute-start | bytes 1179656 | tf_op jit(solution)/shard_map/ppermute | solution.py:82
  58.2 2.3 collective-permute-start.4
  60.9 8.4 %collective-permute-done.4 = bf16[2048,128]{1,0:T(8,128)(2,1)S(1)} collective-permute-done((bf16[2048,128]{1,0:T(8,128)(2,1)S(1)}, bf16[2048,128]{1,0:T(8,128)(2,1)S(1)}, u32[]{:S(2)}, u32[]{:S(2)}) %collective-permute-start.4) | collective-permute-done | bytes 524320 | tf_op jit(solution)/shard_map/ppermute | solution.py:93
  69.5 7.2 %collective-permute-start.5 = (bf16[4096,128]{1,0:T(8,128)(2,1)S(1)}, bf16[4096,128]{1,0:T(8,128)(2,1)}, u32[]{:S(2)}, u32[]{:S(2)}) collective-permute-start(bf16[4096,128]{1,0:T(8,128)(2,1)S(1)} %maximum_select_fusion), channel_id=1, source_target_pairs={{0,1},{1,0},{2,3},{3,2},{4,5},{5,4},{6,7},{7,6},{8,9},{9,8},{10,11... | collective-permute-start | bytes 3145736 | tf_op jit(solution)/shard_map/ppermute | solution.py:97
  78.0 1.9 broadcast_compare_fusion.1
  79.9 2.2 maximum_select_fusion.2
  88.3 12.6 %collective-permute-start.6 = (bf16[8,8,4096]{2,1,0:T(8,128)(2,1)S(1)}, bf16[8,8,4096]{2,1,0:T(8,128)(2,1)S(1)}, u32[]{:S(2)}, u32[]{:S(2)}) collective-permute-start(bf16[8,8,4096]{2,1,0:T(8,128)(2,1)S(1)} %fusion.26), channel_id=1, source_target_pairs={{0,1},{1,0},{2,3},{3,2},{4,5},{5,4},{6,7},{7,6},{8,9},{9,8},{10,11... | collective-permute-start | bytes 1572872 | tf_op jit(solution)/shard_map/ppermute | solution.py:152
  102.6 34.0 %all_to_all.15 = bf16[8,8,4096]{2,1,0:T(8,128)(2,1)S(1)} all-to-all(bf16[8,8,4096]{2,1,0:T(8,128)(2,1)S(1)} %fusion.13), channel_id=1, replica_groups=mesh['zh'=2,'x'=4,'y'=4,'zl'=8,'c'=2] {'zl'}, dimensions={0} | all-to-all | bytes 1048576 | tf_op jit(solution)/shard_map/all_to_all | solution.py:155
  137.0 4.6 %collective-permute-start.8 = (bf16[8,4096]{1,0:T(8,128)(2,1)S(1)}, bf16[8,4096]{1,0:T(8,128)(2,1)S(1)}, u32[]{:S(2)}, u32[]{:S(2)}) collective-permute-start(bf16[8,4096]{1,0:T(8,128)(2,1)S(1)} %fusion.44), channel_id=1, source_target_pairs={{0,8},{2,10},{4,12},{6,14},{8,0},{10,2},{12,4},{14,6},{1,9},{3,11}... | collective-permute-start | bytes 196616 | tf_op jit(solution)/shard_map/ppermute | solution.py:174
  141.6 4.3 %collective-permute-done.8 = bf16[8,4096]{1,0:T(8,128)(2,1)S(1)} collective-permute-done((bf16[8,4096]{1,0:T(8,128)(2,1)S(1)}, bf16[8,4096]{1,0:T(8,128)(2,1)S(1)}, u32[]{:S(2)}, u32[]{:S(2)}) %collective-permute-start.8) | collective-permute-done | bytes 65568 | tf_op jit(solution)/shard_map/ppermute | solution.py:174
  146.0 3.6 %collective-permute-start.9 = (bf16[16,4096]{1,0:T(8,128)(2,1)S(1)}, bf16[16,4096]{1,0:T(8,128)(2,1)S(1)}, u32[]{:S(2)}, u32[]{:S(2)}) collective-permute-start(bf16[16,4096]{1,0:T(8,128)(2,1)S(1)} %maximum_select_fusion.8), channel_id=1, source_target_pairs={{0,4},{2,6},{4,0},{6,2},{8,12},{10,14},{12,8},{14,10},{1,5},{3,7},... | collective-permute-start | bytes 393224 | tf_op jit(solution)/shard_map/ppermute | solution.py:174
  150.4 10.6 %all-to-all-start.1 = ((f32[16,1,128]{2,1,0:T(1,128)}), f32[16,1,128]{2,1,0:T(1,128)S(1)}, u32[]{:S(2)}, u32[]{:S(2)}) async-start(f32[16,1,128]{2,1,0:T(1,128)} %reshape.398), calls=%async_computation.1 | async-start | bytes 16384 | tf_op jit(solution)/shard_map/all_to_all | solution.py:162
  161.0 3.3 %collective-permute-start.10 = (bf16[32,4096]{1,0:T(8,128)(2,1)S(1)}, bf16[32,4096]{1,0:T(8,128)(2,1)S(1)}, u32[]{:S(2)}, u32[]{:S(2)}) collective-permute-start(bf16[32,4096]{1,0:T(8,128)(2,1)S(1)} %maximum_select_fusion.6), channel_id=1, source_target_pairs={{0,2},{2,0},{4,6},{6,4},{8,10},{10,8},{12,14},{14,12},{1,3},{3,1},... | collective-permute-start | bytes 786440 | tf_op jit(solution)/shard_map/ppermute | solution.py:174
  164.6 6.1 %all-to-all-done.1 = f32[16,1,128]{2,1,0:T(1,128)S(1)} async-done(((f32[16,1,128]{2,1,0:T(1,128)}), f32[16,1,128]{2,1,0:T(1,128)S(1)}, u32[]{:S(2)}, u32[]{:S(2)}) %all-to-all-start.1) | async-done | bytes 8224 | tf_op jit(solution)/shard_map/all_to_all | solution.py:162
  172.3 2.6 %collective-permute-start.11 = (bf16[64,4096]{1,0:T(8,128)(2,1)S(1)}, bf16[64,4096]{1,0:T(8,128)(2,1)S(1)}, u32[]{:S(2)}, u32[]{:S(2)}) collective-permute-start(bf16[64,4096]{1,0:T(8,128)(2,1)S(1)} %maximum_select_fusion.4), channel_id=1, source_target_pairs={{0,1},{1,0},{2,3},{3,2},{4,5},{5,4},{6,7},{7,6},{8,9},{9,8},{10,11... | collective-permute-start | bytes 1572872 | tf_op jit(solution)/shard_map/ppermute | solution.py:178
  177.3 20.8 %all-gather.2.cloned.1.call-done = bf16[1536,4096]{1,0:T(8,128)(2,1)} async-done(((bf16[96,4096]{1,0:T(8,128)(2,1)}), bf16[1536,4096]{1,0:T(8,128)(2,1)}) %all-gather.2.cloned.1.call-update) | async-done | bytes 12582928 | tf_op jit(solution)/shard_map/all_gather | solution.py:86
  198.1 6.4 %fusion.94 = f32[1536,128]{1,0:T(8,128)S(1)} fusion(bf16[1536,4096]{1,0:T(8,128)(2,1)} %all-gather.2.cloned.1.call-done, bf16[128,4096]{1,0:T(8,128)(2,1)S(1)} %convolution_convert_fusion), kind=kOutput, calls=%fused_computation.228 | convolution fusion | flops 1610612736 | bytes 14417920 | tf_op jit(solution)/shard_map/fd,sd->fs/dot_general | solution.py:205
  205.6 10.7 %all-to-all-start.2 = ((bf16[16,8,768]{2,1,0:T(8,128)(2,1)}), bf16[16,8,768]{2,1,0:T(8,128)(2,1)S(1)}, u32[]{:S(2)}, u32[]{:S(2)}) async-start(bf16[16,8,768]{2,1,0:T(8,128)(2,1)} %bitcast.50), calls=%async_computation.2 | async-start | bytes 393216 | tf_op jit(solution)/shard_map/all_to_all | solution.py:210
  216.8 14.1 %all-to-all-done.2 = bf16[16,8,768]{2,1,0:T(8,128)(2,1)S(1)} async-done(((bf16[16,8,768]{2,1,0:T(8,128)(2,1)}), bf16[16,8,768]{2,1,0:T(8,128)(2,1)S(1)}, u32[]{:S(2)}, u32[]{:S(2)}) %all-to-all-start.2) | async-done | bytes 196640 | tf_op jit(solution)/shard_map/all_to_all | solution.py:210
  (130 shorter events, 24.8 us)
Async XLA Ops:
  7.2 80.6 %copy-start = (bf16[256,4096]{1,0:T(8,128)(2,1)S(1)}, bf16[256,4096]{1,0:T(8,128)(2,1)}, u32[]{:S(2)}) copy-start(bf16[256,4096]{1,0:T(8,128)(2,1)} %param.17) | copy-start | bytes 6291460
  7.2 53.4 %copy-start.12 = (s32[64]{0:T(128)S(1)}, s32[64]{0:T(128)}, u32[]{:S(2)}) copy-start(s32[64]{0:T(128)} %param.16) | copy-start | bytes 772
  7.2 190.9 %all-gather.2.cloned.1.call-start = ((), (), s32[]{:S(2)}) async-start(), calls=%async_computation.3 | async-start | bytes 13369344 | tf_op jit(solution)/shard_map/all_gather | solution.py:86
  8.2 17.7 %collective-permute-start = (bf16[128,128]{1,0:T(8,128)(2,1)S(1)}, bf16[128,128]{1,0:T(8,128)(2,1)S(1)}, u32[]{:S(2)}, u32[]{:S(2)}) collective-permute-start(bf16[128,128]{1,0:T(8,128)(2,1)S(1)} %dynamic-slice_select_fusion), channel_id=1, source_target_pairs={{0,256},{16,272},{32,288},{48,304},{64,320},{80,336},{96,352},{112... | collective-permute-start | bytes 98312 | tf_op jit(solution)/shard_map/ppermute | solution.py:81
  25.9 6.5 %collective-permute-start.1 = (bf16[256,128]{1,0:T(8,128)(2,1)S(1)}, bf16[256,128]{1,0:T(8,128)(2,1)S(1)}, u32[]{:S(2)}, u32[]{:S(2)}) collective-permute-start(bf16[256,128]{1,0:T(8,128)(2,1)S(1)} %maximum_select_fusion.9), channel_id=1, source_target_pairs={{0,128},{16,144},{32,160},{48,176},{64,192},{80,208},{96,224},{112... | collective-permute-start | bytes 196616 | tf_op jit(solution)/shard_map/ppermute | solution.py:93
  32.4 5.7 %collective-permute-start.2 = (bf16[512,128]{1,0:T(8,128)(2,1)S(1)}, bf16[512,128]{1,0:T(8,128)(2,1)S(1)}, u32[]{:S(2)}, u32[]{:S(2)}) collective-permute-start(bf16[512,128]{1,0:T(8,128)(2,1)S(1)} %maximum_select_fusion.7), channel_id=1, source_target_pairs={{0,64},{16,80},{32,96},{48,112},{64,0},{80,16},{96,32},{112,48},{1... | collective-permute-start | bytes 393224 | tf_op jit(solution)/shard_map/ppermute | solution.py:93
  38.2 19.9 %collective-permute-start.3 = (bf16[1024,128]{1,0:T(8,128)(2,1)S(1)}, bf16[1024,128]{1,0:T(8,128)(2,1)S(1)}, u32[]{:S(2)}, u32[]{:S(2)}) collective-permute-start(bf16[1024,128]{1,0:T(8,128)(2,1)S(1)} %maximum_select_fusion.5), channel_id=1, source_target_pairs={{0,32},{16,48},{32,0},{48,16},{64,96},{80,112},{96,64},{112,80},{1... | collective-permute-start | bytes 786440 | tf_op jit(solution)/shard_map/ppermute | solution.py:93
  44.9 35.0 %copy-start.1 = (bf16[1,4096,24]{1,2,0:T(8,128)(2,1)S(1)}, bf16[1,4096,24]{1,2,0:T(8,128)(2,1)}, u32[]{:S(2)}) copy-start(bf16[1,4096,24]{1,2,0:T(8,128)(2,1)} %param.20) | copy-start | bytes 589828
  44.9 35.0 %copy-start.2 = (bf16[1,4096,24]{1,2,0:T(8,128)(2,1)S(1)}, bf16[1,4096,24]{1,2,0:T(8,128)(2,1)}, u32[]{:S(2)}) copy-start(bf16[1,4096,24]{1,2,0:T(8,128)(2,1)} %param.19) | copy-start | bytes 589828
  44.9 35.0 %collective-permute-start.7 = (bf16[48,4096]{1,0:T(8,128)(2,1)}, bf16[48,4096]{1,0:T(8,128)(2,1)}, u32[]{:S(2)}, u32[]{:S(2)}) collective-permute-start(bf16[48,4096]{1,0:T(8,128)(2,1)} %pad_maximum_fusion), channel_id=1, source_target_pairs={{0,256},{256,0},{1,257},{257,1},{2,258},{258,2},{3,259},{259,3},{4... | collective-permute-start | bytes 1179656 | tf_op jit(solution)/shard_map/ppermute | solution.py:82
  58.2 11.0 %collective-permute-start.4 = (bf16[2048,128]{1,0:T(8,128)(2,1)S(1)}, bf16[2048,128]{1,0:T(8,128)(2,1)S(1)}, u32[]{:S(2)}, u32[]{:S(2)}) collective-permute-start(bf16[2048,128]{1,0:T(8,128)(2,1)S(1)} %maximum_select_fusion.3), channel_id=1, source_target_pairs={{0,16},{16,0},{32,48},{48,32},{64,80},{80,64},{96,112},{112,96},{1... | collective-permute-start | bytes 1572872 | tf_op jit(solution)/shard_map/ppermute | solution.py:93
  69.5 12.7 %collective-permute-start.5 = (bf16[4096,128]{1,0:T(8,128)(2,1)S(1)}, bf16[4096,128]{1,0:T(8,128)(2,1)}, u32[]{:S(2)}, u32[]{:S(2)}) collective-permute-start(bf16[4096,128]{1,0:T(8,128)(2,1)S(1)} %maximum_select_fusion), channel_id=1, source_target_pairs={{0,1},{1,0},{2,3},{3,2},{4,5},{5,4},{6,7},{7,6},{8,9},{9,8},{10,11... | collective-permute-start | bytes 3145736 | tf_op jit(solution)/shard_map/ppermute | solution.py:97
  88.3 48.5 %copy-start.8 = (bf16[8,4096]{1,0:T(8,128)(2,1)S(1)}, bf16[8,4096]{1,0:T(8,128)(2,1)}, u32[]{:S(2)}) copy-start(bf16[8,4096]{1,0:T(8,128)(2,1)} %param.12) | copy-start | bytes 196612
  88.3 48.6 %copy-start.10 = (f32[4096]{0:T(1024)S(1)}, f32[4096]{0:T(1024)}, u32[]{:S(2)}) copy-start(f32[4096]{0:T(1024)} %param.18) | copy-start | bytes 49156
  88.3 61.3 %copy-start.9 = (s32[8,8]{1,0:T(8,128)S(1)}, s32[8,8]{1,0:T(8,128)}, u32[]{:S(2)}) copy-start(s32[8,8]{1,0:T(8,128)} %param.21) | copy-start | bytes 772
  88.3 61.3 %copy-start.11 = (f32[8,8]{1,0:T(8,128)S(1)}, f32[8,8]{1,0:T(8,128)}, u32[]{:S(2)}) copy-start(f32[8,8]{1,0:T(8,128)} %param.22) | copy-start | bytes 772
  88.3 14.1 %collective-permute-start.6 = (bf16[8,8,4096]{2,1,0:T(8,128)(2,1)S(1)}, bf16[8,8,4096]{2,1,0:T(8,128)(2,1)S(1)}, u32[]{:S(2)}, u32[]{:S(2)}) collective-permute-start(bf16[8,8,4096]{2,1,0:T(8,128)(2,1)S(1)} %fusion.26), channel_id=1, source_target_pairs={{0,1},{1,0},{2,3},{3,2},{4,5},{5,4},{6,7},{7,6},{8,9},{9,8},{10,11... | collective-permute-start | bytes 1572872 | tf_op jit(solution)/shard_map/ppermute | solution.py:152
  136.9 39.7 %copy-start.7 = (bf16[8,4096]{1,0:T(8,128)(2,1)}, bf16[8,4096]{1,0:T(8,128)(2,1)S(1)}, u32[]{:S(2)}) copy-start(bf16[8,4096]{1,0:T(8,128)(2,1)S(1)} %get-tuple-element.9) | copy-start | bytes 196612
  137.0 8.9 %collective-permute-start.8 = (bf16[8,4096]{1,0:T(8,128)(2,1)S(1)}, bf16[8,4096]{1,0:T(8,128)(2,1)S(1)}, u32[]{:S(2)}, u32[]{:S(2)}) collective-permute-start(bf16[8,4096]{1,0:T(8,128)(2,1)S(1)} %fusion.44), channel_id=1, source_target_pairs={{0,8},{2,10},{4,12},{6,14},{8,0},{10,2},{12,4},{14,6},{1,9},{3,11}... | collective-permute-start | bytes 196616 | tf_op jit(solution)/shard_map/ppermute | solution.py:174
  146.0 15.0 %collective-permute-start.9 = (bf16[16,4096]{1,0:T(8,128)(2,1)S(1)}, bf16[16,4096]{1,0:T(8,128)(2,1)S(1)}, u32[]{:S(2)}, u32[]{:S(2)}) collective-permute-start(bf16[16,4096]{1,0:T(8,128)(2,1)S(1)} %maximum_select_fusion.8), channel_id=1, source_target_pairs={{0,4},{2,6},{4,0},{6,2},{8,12},{10,14},{12,8},{14,10},{1,5},{3,7},... | collective-permute-start | bytes 393224 | tf_op jit(solution)/shard_map/ppermute | solution.py:174
  150.4 20.3 %all-to-all-start.1 = ((f32[16,1,128]{2,1,0:T(1,128)}), f32[16,1,128]{2,1,0:T(1,128)S(1)}, u32[]{:S(2)}, u32[]{:S(2)}) async-start(f32[16,1,128]{2,1,0:T(1,128)} %reshape.398), calls=%async_computation.1 | async-start | bytes 16384 | tf_op jit(solution)/shard_map/all_to_all | solution.py:162
  161.0 11.1 %collective-permute-start.10 = (bf16[32,4096]{1,0:T(8,128)(2,1)S(1)}, bf16[32,4096]{1,0:T(8,128)(2,1)S(1)}, u32[]{:S(2)}, u32[]{:S(2)}) collective-permute-start(bf16[32,4096]{1,0:T(8,128)(2,1)S(1)} %maximum_select_fusion.6), channel_id=1, source_target_pairs={{0,2},{2,0},{4,6},{6,4},{8,10},{10,8},{12,14},{14,12},{1,3},{3,1},... | collective-permute-start | bytes 786440 | tf_op jit(solution)/shard_map/ppermute | solution.py:174
  172.3 4.1 %collective-permute-start.11 = (bf16[64,4096]{1,0:T(8,128)(2,1)S(1)}, bf16[64,4096]{1,0:T(8,128)(2,1)S(1)}, u32[]{:S(2)}, u32[]{:S(2)}) collective-permute-start(bf16[64,4096]{1,0:T(8,128)(2,1)S(1)} %maximum_select_fusion.4), channel_id=1, source_target_pairs={{0,1},{1,0},{2,3},{3,2},{4,5},{5,4},{6,7},{7,6},{8,9},{9,8},{10,11... | collective-permute-start | bytes 1572872 | tf_op jit(solution)/shard_map/ppermute | solution.py:178
  205.6 25.3 %all-to-all-start.2 = ((bf16[16,8,768]{2,1,0:T(8,128)(2,1)}), bf16[16,8,768]{2,1,0:T(8,128)(2,1)S(1)}, u32[]{:S(2)}, u32[]{:S(2)}) async-start(bf16[16,8,768]{2,1,0:T(8,128)(2,1)} %bitcast.50), calls=%async_computation.2 | async-start | bytes 393216 | tf_op jit(solution)/shard_map/all_to_all | solution.py:210
  (5 other events, 7.3 us)
Sparse Core Ops, SparseCore 0:
  82.2 115.8 all-gather.1
where the time goes:
time: 240 us; the launch traced here: 239 us
  starting transfers between devices  98.8 us (41%)
  waiting for transfers between devices  62.1 us (26%)
  blocking collectives  34 us (14%)
  other arithmetic  15.4 us (6%)
  between operations  14.8 us (6%)
  matrix products  10.1 us (4%)
  local copies, waits for them, and re-layouts  3.99 us (2%)
    all_to_all x1, blocking collectives, shards(): lax.all_to_all(pair_sum, 'zl', split_axis=0, concat_axis=0, tiled=True)  34 us
    all_gather x1, waiting for transfers between devices, shards(): w_all = lax.all_gather(w_pair, ('x', 'y'), axis=0, tiled=True)  20.8 us
    ppermute x1, starting transfers between devices, shards(): lax.ppermute(kv_local, CTX, [(i, i ^ first) for i in range(n_ctx)])  16.3 us
    ppermute x4, starting transfers between devices, shards(): other = lax.ppermute(cur, CTX, [(i, i ^ bit) for i in range(n_ctx)])  14.9 us
    all_to_all x1, waiting for transfers between devices, shards(): lax.all_to_all(hidden, EXP, split_axis=0, concat_axis=0, tiled=True)  14.1 us
    ppermute x4, waiting for transfers between devices, shards(): other = lax.ppermute(cur, CTX, [(i, i ^ bit) for i in range(n_ctx)])  12.8 us
    ppermute x1, starting transfers between devices, shards(): got = lax.ppermute(give, 'c', [(0, 1), (1, 0)])  12.6 us
    ppermute x1, starting transfers between devices, shards(): w_other = lax.ppermute(w_local, 'zh', [(0, 1), (1, 0)])  12.5 us
  transfers between devices with their start and end apart: 15, of which 10 were waited for; matrix products, arithmetic and copies ran while one was open for 8% of the time, Pallas kernels for 0%

commit v1 on v0

--- a/solution.py
+++ b/solution.py
@@ -83,7 +83,20 @@
     w_pair = jnp.where(
         zh_index == 0, jnp.concatenate([w_local, w_other]), jnp.concatenate([w_other, w_local])
     )
-    w_all = lax.all_gather(w_pair, ("x", "y"), axis=0, tiled=True)
+
+    def test_grid(here_x):
+        clean = jnp.concatenate(
+            lax.all_to_all(
+                jnp.stack([here_x for _ in range(lax.psum(1, axis_name=("x", "y")))], axis=0),
+                axis_name=("x", "y"),
+                split_axis=0,
+                concat_axis=0,
+            ),
+            axis=0,
+        )
+        return clean
+
+    w_all = test_grid(w_pair)
     low = ctx_index & first == 0
     cur = jnp.where(
         low, jnp.concatenate([kv_local, kv_other]), jnp.concatenate([kv_other, kv_local])

time: 240 us -> 454 us (1.89)
  waiting for transfers between devices: 62.1 us -> 290 us
  blocking collectives: 34 us -> 0 us
  starting transfers between devices: 98.8 us -> 128 us
  between operations: 14.8 us -> 1.39 us
  local copies, waits for them, and re-layouts: 3.99 us -> 9.85 us
    all_to_all x0 -> x2, waiting for transfers between devices: none -> 249 us  [the longest x1 217 us: test_grid(): lax.all_to_all(jnp.stack([here_x for _ in range(lax.psum(1, axis_name=('x...]
    all_to_all x1 -> x0, blocking collectives: 34 us -> none  [shards(): lax.all_to_all(pair_sum, 'zl', split_axis=0, concat_axis=0, tiled=True)]
    all_gather x1 -> x0, waiting for transfers between devices: 20.8 us -> none  [shards(): w_all = lax.all_gather(w_pair, ('x', 'y'), axis=0, tiled=True)]
    all_to_all x1, starting transfers between devices: 10.6 us -> 24.9 us  [shards(): lax.all_to_all(jnp.broadcast_to(ids_rw[None], (n_exp,) + ids_rw.shape), E...]
    all_to_all x0 -> x2, starting transfers between devices: none -> 14.2 us  [the longest x1 7.36 us: shards(): lax.all_to_all(pair_sum, 'zl', split_axis=0, concat_axis=0, tiled=True)]
    ppermute x1, starting transfers between devices: 12.6 us -> 2.4 us  [shards(): got = lax.ppermute(give, 'c', [(0, 1), (1, 0)])]
    ppermute x3, starting transfers between devices: 11.5 us -> 19.9 us  [shards(): other = lax.ppermute(cur, 'zl', [(i, i ^ bit) for i in range(n_zl)])]
    another operation x0 -> x1, local copies, waits for them, and re-layouts: none -> 6.06 us  [test_grid(): jnp.stack([here_x for _ in range(lax.psum(1, axis_name=('x', 'y')))], axi...]
  transfers between devices with their start and end apart: 15 -> 16, of which waited for: 10 -> 13; matrix products, arithmetic and copies ran while one was open for 8% -> 4% of each run, Pallas kernels for 0% -> 0%
where the time goes in v1:
time: 454 us; the launch traced here: 453 us
  waiting for transfers between devices  290 us (64%)
  starting transfers between devices  128 us (28%)
  other arithmetic  12.5 us (3%)
  matrix products  10.1 us (2%)
  local copies, waits for them, and re-layouts  9.85 us (2%)
    all_to_all x1, waiting for transfers between devices, test_grid(): lax.all_to_all(jnp.stack([here_x for _ in range(lax.psum(1, axis_name=('x...  217 us
    all_to_all x1, waiting for transfers between devices, shards(): lax.all_to_all(pair_sum, 'zl', split_axis=0, concat_axis=0, tiled=True)  32.7 us
    all_to_all x1, starting transfers between devices, shards(): lax.all_to_all(jnp.broadcast_to(ids_rw[None], (n_exp,) + ids_rw.shape), E...  24.9 us
    ppermute x3, starting transfers between devices, shards(): other = lax.ppermute(cur, 'zl', [(i, i ^ bit) for i in range(n_zl)])  19.9 us
    ppermute x1, starting transfers between devices, shards(): lax.ppermute(kv_local, CTX, [(i, i ^ first) for i in range(n_ctx)])  16.3 us
    ppermute x4, starting transfers between devices, shards(): other = lax.ppermute(cur, CTX, [(i, i ^ bit) for i in range(n_ctx)])  15.8 us
    ppermute x4, waiting for transfers between devices, shards(): other = lax.ppermute(cur, CTX, [(i, i ^ bit) for i in range(n_ctx)])  14.8 us
    ppermute x2, starting transfers between devices, shards(): partner = lax.ppermute(cur, 'c', [(0, 1), (1, 0)])  14.3 us
  transfers between devices with their start and end apart: 16, of which 13 were waited for; matrix products, arithmetic and copies ran while one was open for 4% of the time, Pallas kernels for 0%

profile of v1, /device:TPU:1, one launch (start us, length us, event | category | flops | bytes accessed | tf_op | source)
XLA Modules:
  0.0 452.5 jit_solution(1621672449711888879)
XLA Ops:
  1.6 16.3 %collective-permute-start = (bf16[128,128]{1,0:T(8,128)(2,1)S(1)}, bf16[128,128]{1,0:T(8,128)(2,1)S(1)}, u32[]{:S(2)}, u32[]{:S(2)}) collective-permute-start(bf16[128,128]{1,0:T(8,128)(2,1)S(1)} %dynamic-slice_select_fusion), channel_id=1, source_target_pairs={{0,256},{16,272},{32,288},{48,304},{64,320},{80,336},{96,352},{112... | collective-permute-start | bytes 98312 | tf_op jit(solution)/shard_map/ppermute | solution.py:81
  19.3 4.7 %collective-permute-start.1 = (bf16[256,128]{1,0:T(8,128)(2,1)S(1)}, bf16[256,128]{1,0:T(8,128)(2,1)S(1)}, u32[]{:S(2)}, u32[]{:S(2)}) collective-permute-start(bf16[256,128]{1,0:T(8,128)(2,1)S(1)} %maximum_select_fusion.9), channel_id=1, source_target_pairs={{0,128},{16,144},{32,160},{48,176},{64,192},{80,208},{96,224},{112... | collective-permute-start | bytes 196616 | tf_op jit(solution)/shard_map/ppermute | solution.py:106
  25.9 3.1 collective-permute-start.2
  29.0 2.6 collective-permute-done.2
  31.7 4.8 %collective-permute-start.3 = (bf16[1024,128]{1,0:T(8,128)(2,1)S(1)}, bf16[1024,128]{1,0:T(8,128)(2,1)S(1)}, u32[]{:S(2)}, u32[]{:S(2)}) collective-permute-start(bf16[1024,128]{1,0:T(8,128)(2,1)S(1)} %maximum_select_fusion.5), channel_id=1, source_target_pairs={{0,32},{16,48},{32,0},{48,16},{64,96},{80,112},{96,64},{112,80},{1... | collective-permute-start | bytes 786440 | tf_op jit(solution)/shard_map/ppermute | solution.py:106
  36.5 3.8 collective-permute-done.3
  40.4 3.2 collective-permute-start.4
  43.8 6.6 %collective-permute-done.4 = bf16[2048,128]{1,0:T(8,128)(2,1)S(1)} collective-permute-done((bf16[2048,128]{1,0:T(8,128)(2,1)S(1)}, bf16[2048,128]{1,0:T(8,128)(2,1)S(1)}, u32[]{:S(2)}, u32[]{:S(2)}) %collective-permute-start.4) | collective-permute-done | bytes 524320 | tf_op jit(solution)/shard_map/ppermute | solution.py:106
  50.7 10.1 %collective-permute-start.5 = (bf16[4096,128]{1,0:T(8,128)(2,1)S(1)}, bf16[4096,128]{1,0:T(8,128)(2,1)S(1)}, u32[]{:S(2)}, u32[]{:S(2)}) collective-permute-start(bf16[4096,128]{1,0:T(8,128)(2,1)S(1)} %maximum_select_fusion), channel_id=1, source_target_pairs={{0,1},{1,0},{2,3},{3,2},{4,5},{5,4},{6,7},{7,6},{8,9},{9,8},{10,11... | collective-permute-start | bytes 3145736 | tf_op jit(solution)/shard_map/ppermute | solution.py:110
  72.6 7.4 %all-to-all-start = ((bf16[8,8,4096]{2,1,0:T(8,128)(2,1)}), bf16[8,8,4096]{2,1,0:T(8,128)(2,1)S(1)}, u32[]{:S(2)}, u32[]{:S(2)}) async-start(bf16[8,8,4096]{2,1,0:T(8,128)(2,1)} %fusion.15), calls=%async_computation | async-start | bytes 1048576 | tf_op jit(solution)/shard_map/all_to_all | solution.py:168
  80.0 8.2 %collective-permute-start.7 = (bf16[48,4096]{1,0:T(8,128)(2,1)S(1)}, bf16[48,4096]{1,0:T(8,128)(2,1)}, u32[]{:S(2)}, u32[]{:S(2)}) collective-permute-start(bf16[48,4096]{1,0:T(8,128)(2,1)S(1)} %pad_maximum_fusion), channel_id=1, source_target_pairs={{0,256},{256,0},{1,257},{257,1},{2,258},{258,2},{3,259},{259,3},{4... | collective-permute-start | bytes 1179656 | tf_op jit(solution)/shard_map/ppermute | solution.py:82
  89.0 32.7 %all-to-all-done = bf16[8,8,4096]{2,1,0:T(8,128)(2,1)S(1)} async-done(((bf16[8,8,4096]{2,1,0:T(8,128)(2,1)}), bf16[8,8,4096]{2,1,0:T(8,128)(2,1)S(1)}, u32[]{:S(2)}, u32[]{:S(2)}) %all-to-all-start) | async-done | bytes 524320 | tf_op jit(solution)/shard_map/all_to_all | solution.py:168
  121.7 24.9 %all-to-all-start.2 = ((f32[16,1,128]{2,1,0:T(1,128)}), f32[16,1,128]{2,1,0:T(1,128)S(1)}, u32[]{:S(2)}, u32[]{:S(2)}) async-start(f32[16,1,128]{2,1,0:T(1,128)} %reshape.418), calls=%async_computation.2 | async-start | bytes 16384 | tf_op jit(solution)/shard_map/all_to_all | solution.py:175
  147.7 7.2 %collective-permute-start.8 = (bf16[8,4096]{1,0:T(8,128)(2,1)S(1)}, bf16[8,4096]{1,0:T(8,128)(2,1)S(1)}, u32[]{:S(2)}, u32[]{:S(2)}) collective-permute-start(bf16[8,4096]{1,0:T(8,128)(2,1)S(1)} %fusion.47), channel_id=1, source_target_pairs={{0,8},{2,10},{4,12},{6,14},{8,0},{10,2},{12,4},{14,6},{1,9},{3,11}... | collective-permute-start | bytes 196616 | tf_op jit(solution)/shard_map/ppermute | solution.py:187
  157.7 5.9 %collective-permute-start.9 = (bf16[16,4096]{1,0:T(8,128)(2,1)S(1)}, bf16[16,4096]{1,0:T(8,128)(2,1)S(1)}, u32[]{:S(2)}, u32[]{:S(2)}) collective-permute-start(bf16[16,4096]{1,0:T(8,128)(2,1)S(1)} %maximum_select_fusion.8), channel_id=1, source_target_pairs={{0,4},{2,6},{4,0},{6,2},{8,12},{10,14},{12,8},{14,10},{1,5},{3,7},... | collective-permute-start | bytes 393224 | tf_op jit(solution)/shard_map/ppermute | solution.py:187
  166.1 6.7 %collective-permute-start.10 = (bf16[32,4096]{1,0:T(8,128)(2,1)S(1)}, bf16[32,4096]{1,0:T(8,128)(2,1)}, u32[]{:S(2)}, u32[]{:S(2)}) collective-permute-start(bf16[32,4096]{1,0:T(8,128)(2,1)S(1)} %maximum_select_fusion.6), channel_id=1, source_target_pairs={{0,2},{2,0},{4,6},{6,4},{8,10},{10,8},{12,14},{14,12},{1,3},{3,1},... | collective-permute-start | bytes 786440 | tf_op jit(solution)/shard_map/ppermute | solution.py:187
  173.2 4.7 %collective-permute-done.10 = bf16[32,4096]{1,0:T(8,128)(2,1)} collective-permute-done((bf16[32,4096]{1,0:T(8,128)(2,1)S(1)}, bf16[32,4096]{1,0:T(8,128)(2,1)}, u32[]{:S(2)}, u32[]{:S(2)}) %collective-permute-start.10) | collective-permute-done | bytes 262176 | tf_op jit(solution)/shard_map/ppermute | solution.py:187
  179.1 4.1 collective-permute-start.11
  184.9 6.1 %stack.2 = bf16[16,96,4096]{2,1,0:T(8,128)(2,1)} broadcast(bf16[96,4096]{1,0:T(8,128)(2,1)S(1)} %maximum_select_fusion.2), dimensions={1,2} | broadcast | bytes 13369344 | tf_op jit(solution)/shard_map/stack | solution.py:90
  191.0 6.8 %all-to-all-start.1 = ((bf16[16,96,4096]{2,1,0:T(8,128)(2,1)}), bf16[16,96,4096]{2,1,0:T(8,128)(2,1)}, u32[]{:S(2)}, u32[]{:S(2)}) async-start(bf16[16,96,4096]{2,1,0:T(8,128)(2,1)} %stack.2), calls=%async_computation.1 | async-start | bytes 25165824 | tf_op jit(solution)/shard_map/all_to_all | solution.py:89
  200.0 216.5 %all-to-all-done.1 = bf16[16,96,4096]{2,1,0:T(8,128)(2,1)} async-done(((bf16[16,96,4096]{2,1,0:T(8,128)(2,1)}), bf16[16,96,4096]{2,1,0:T(8,128)(2,1)}, u32[]{:S(2)}, u32[]{:S(2)}) %all-to-all-start.1) | async-done | bytes 12582944 | tf_op jit(solution)/shard_map/all_to_all | solution.py:89
  416.5 6.4 %fusion.13 = f32[16,2,2,24,128]{4,3,2,1,0:T(8,128)S(1)} fusion(bf16[16,2,2,24,4096]{4,3,2,1,0:T(8,128)(2,1)} %bitcast.43, bf16[128,4096]{1,0:T(8,128)(2,1)S(1)} %convolution_convert_fusion), kind=kOutput, calls=%fused_computation.26 | convolution fusion | flops 1610612736 | bytes 14417920 | tf_op jit(solution)/shard_map/fd,sd->fs/dot_general | solution.py:218
  424.0 12.5 %all-to-all-start.3 = ((bf16[16,8,768]{2,1,0:T(8,128)(2,1)}), bf16[16,8,768]{2,1,0:T(8,128)(2,1)S(1)}, u32[]{:S(2)}, u32[]{:S(2)}) async-start(bf16[16,8,768]{2,1,0:T(8,128)(2,1)} %bitcast.52), calls=%async_computation.3 | async-start | bytes 393216 | tf_op jit(solution)/shard_map/all_to_all | solution.py:223
  437.0 14.1 %all-to-all-done.3 = bf16[16,8,768]{2,1,0:T(8,128)(2,1)S(1)} async-done(((bf16[16,8,768]{2,1,0:T(8,128)(2,1)}), bf16[16,8,768]{2,1,0:T(8,128)(2,1)S(1)}, u32[]{:S(2)}, u32[]{:S(2)}) %all-to-all-start.3) | async-done | bytes 196640 | tf_op jit(solution)/shard_map/all_to_all | solution.py:223
  (123 shorter events, 31.7 us)
Async XLA Ops:
  0.6 66.5 %copy-start = (bf16[256,4096]{1,0:T(8,128)(2,1)S(1)}, bf16[256,4096]{1,0:T(8,128)(2,1)}, u32[]{:S(2)}) copy-start(bf16[256,4096]{1,0:T(8,128)(2,1)} %param.17) | copy-start | bytes 6291460
  0.6 43.1 %copy-start.8 = (s32[32]{0:T(128)S(1)}, s32[32]{0:T(128)}, u32[]{:S(2)}) copy-start(s32[32]{0:T(128)} %constant.185) | copy-start | bytes 388
  0.7 43.0 %copy-start.7 = (s32[64]{0:T(128)S(1)}, s32[64]{0:T(128)}, u32[]{:S(2)}) copy-start(s32[64]{0:T(128)} %param.16) | copy-start | bytes 772
  1.6 17.7 %collective-permute-start = (bf16[128,128]{1,0:T(8,128)(2,1)S(1)}, bf16[128,128]{1,0:T(8,128)(2,1)S(1)}, u32[]{:S(2)}, u32[]{:S(2)}) collective-permute-start(bf16[128,128]{1,0:T(8,128)(2,1)S(1)} %dynamic-slice_select_fusion), channel_id=1, source_target_pairs={{0,256},{16,272},{32,288},{48,304},{64,320},{80,336},{96,352},{112... | collective-permute-start | bytes 98312 | tf_op jit(solution)/shard_map/ppermute | solution.py:81
  19.3 6.5 %collective-permute-start.1 = (bf16[256,128]{1,0:T(8,128)(2,1)S(1)}, bf16[256,128]{1,0:T(8,128)(2,1)S(1)}, u32[]{:S(2)}, u32[]{:S(2)}) collective-permute-start(bf16[256,128]{1,0:T(8,128)(2,1)S(1)} %maximum_select_fusion.9), channel_id=1, source_target_pairs={{0,128},{16,144},{32,160},{48,176},{64,192},{80,208},{96,224},{112... | collective-permute-start | bytes 196616 | tf_op jit(solution)/shard_map/ppermute | solution.py:106
  25.9 5.7 %collective-permute-start.2 = (bf16[512,128]{1,0:T(8,128)(2,1)S(1)}, bf16[512,128]{1,0:T(8,128)(2,1)S(1)}, u32[]{:S(2)}, u32[]{:S(2)}) collective-permute-start(bf16[512,128]{1,0:T(8,128)(2,1)S(1)} %maximum_select_fusion.7), channel_id=1, source_target_pairs={{0,64},{16,80},{32,96},{48,112},{64,0},{80,16},{96,32},{112,48},{1... | collective-permute-start | bytes 393224 | tf_op jit(solution)/shard_map/ppermute | solution.py:106
  31.7 8.6 %collective-permute-start.3 = (bf16[1024,128]{1,0:T(8,128)(2,1)S(1)}, bf16[1024,128]{1,0:T(8,128)(2,1)S(1)}, u32[]{:S(2)}, u32[]{:S(2)}) collective-permute-start(bf16[1024,128]{1,0:T(8,128)(2,1)S(1)} %maximum_select_fusion.5), channel_id=1, source_target_pairs={{0,32},{16,48},{32,0},{48,16},{64,96},{80,112},{96,64},{112,80},{1... | collective-permute-start | bytes 786440 | tf_op jit(solution)/shard_map/ppermute | solution.py:106
  40.4 10.0 %collective-permute-start.4 = (bf16[2048,128]{1,0:T(8,128)(2,1)S(1)}, bf16[2048,128]{1,0:T(8,128)(2,1)S(1)}, u32[]{:S(2)}, u32[]{:S(2)}) collective-permute-start(bf16[2048,128]{1,0:T(8,128)(2,1)S(1)} %maximum_select_fusion.3), channel_id=1, source_target_pairs={{0,16},{16,0},{32,48},{48,32},{64,80},{80,64},{96,112},{112,96},{1... | collective-permute-start | bytes 1572872 | tf_op jit(solution)/shard_map/ppermute | solution.py:106
  50.7 12.4 %collective-permute-start.5 = (bf16[4096,128]{1,0:T(8,128)(2,1)S(1)}, bf16[4096,128]{1,0:T(8,128)(2,1)S(1)}, u32[]{:S(2)}, u32[]{:S(2)}) collective-permute-start(bf16[4096,128]{1,0:T(8,128)(2,1)S(1)} %maximum_select_fusion), channel_id=1, source_target_pairs={{0,1},{1,0},{2,3},{3,2},{4,5},{5,4},{6,7},{7,6},{8,9},{9,8},{10,11... | collective-permute-start | bytes 3145736 | tf_op jit(solution)/shard_map/ppermute | solution.py:110
  67.6 12.4 %copy-start.1 = (bf16[1,4096,24]{1,2,0:T(8,128)(2,1)S(1)}, bf16[1,4096,24]{1,2,0:T(8,128)(2,1)}, u32[]{:S(2)}) copy-start(bf16[1,4096,24]{1,2,0:T(8,128)(2,1)} %param.20) | copy-start | bytes 589828
  67.7 20.5 %copy-start.5 = (s32[8,8]{1,0:T(8,128)S(1)}, s32[8,8]{1,0:T(8,128)}, u32[]{:S(2)}) copy-start(s32[8,8]{1,0:T(8,128)} %param.21) | copy-start | bytes 772
  67.7 20.5 %copy-start.6 = (f32[8,8]{1,0:T(8,128)S(1)}, f32[8,8]{1,0:T(8,128)}, u32[]{:S(2)}) copy-start(f32[8,8]{1,0:T(8,128)} %param.22) | copy-start | bytes 772
  67.7 79.0 %copy-start.4 = (bf16[8,4096]{1,0:T(8,128)(2,1)S(1)}, bf16[8,4096]{1,0:T(8,128)(2,1)}, u32[]{:S(2)}) copy-start(bf16[8,4096]{1,0:T(8,128)(2,1)} %param.12) | copy-start | bytes 196612
  67.7 3.9 collective-permute-start.6
  72.6 49.1 %all-to-all-start = ((bf16[8,8,4096]{2,1,0:T(8,128)(2,1)}), bf16[8,8,4096]{2,1,0:T(8,128)(2,1)S(1)}, u32[]{:S(2)}, u32[]{:S(2)}) async-start(bf16[8,8,4096]{2,1,0:T(8,128)(2,1)} %fusion.15), calls=%async_computation | async-start | bytes 1048576 | tf_op jit(solution)/shard_map/all_to_all | solution.py:168
  80.0 103.3 %collective-permute-start.7 = (bf16[48,4096]{1,0:T(8,128)(2,1)S(1)}, bf16[48,4096]{1,0:T(8,128)(2,1)}, u32[]{:S(2)}, u32[]{:S(2)}) collective-permute-start(bf16[48,4096]{1,0:T(8,128)(2,1)S(1)} %pad_maximum_fusion), channel_id=1, source_target_pairs={{0,256},{256,0},{1,257},{257,1},{2,258},{258,2},{3,259},{259,3},{4... | collective-permute-start | bytes 1179656 | tf_op jit(solution)/shard_map/ppermute | solution.py:82
  121.7 34.7 %all-to-all-start.2 = ((f32[16,1,128]{2,1,0:T(1,128)}), f32[16,1,128]{2,1,0:T(1,128)S(1)}, u32[]{:S(2)}, u32[]{:S(2)}) async-start(f32[16,1,128]{2,1,0:T(1,128)} %reshape.418), calls=%async_computation.2 | async-start | bytes 16384 | tf_op jit(solution)/shard_map/all_to_all | solution.py:175
  146.9 44.2 %copy-start.3 = (bf16[8,4096]{1,0:T(8,128)(2,1)}, bf16[8,4096]{1,0:T(8,128)(2,1)S(1)}, u32[]{:S(2)}) copy-start(bf16[8,4096]{1,0:T(8,128)(2,1)S(1)} %get-tuple-element.9) | copy-start | bytes 196612
  147.7 10.0 %collective-permute-start.8 = (bf16[8,4096]{1,0:T(8,128)(2,1)S(1)}, bf16[8,4096]{1,0:T(8,128)(2,1)S(1)}, u32[]{:S(2)}, u32[]{:S(2)}) collective-permute-start(bf16[8,4096]{1,0:T(8,128)(2,1)S(1)} %fusion.47), channel_id=1, source_target_pairs={{0,8},{2,10},{4,12},{6,14},{8,0},{10,2},{12,4},{14,6},{1,9},{3,11}... | collective-permute-start | bytes 196616 | tf_op jit(solution)/shard_map/ppermute | solution.py:187
  157.7 8.3 %collective-permute-start.9 = (bf16[16,4096]{1,0:T(8,128)(2,1)S(1)}, bf16[16,4096]{1,0:T(8,128)(2,1)S(1)}, u32[]{:S(2)}, u32[]{:S(2)}) collective-permute-start(bf16[16,4096]{1,0:T(8,128)(2,1)S(1)} %maximum_select_fusion.8), channel_id=1, source_target_pairs={{0,4},{2,6},{4,0},{6,2},{8,12},{10,14},{12,8},{14,10},{1,5},{3,7},... | collective-permute-start | bytes 393224 | tf_op jit(solution)/shard_map/ppermute | solution.py:187
  166.1 11.9 %collective-permute-start.10 = (bf16[32,4096]{1,0:T(8,128)(2,1)S(1)}, bf16[32,4096]{1,0:T(8,128)(2,1)}, u32[]{:S(2)}, u32[]{:S(2)}) collective-permute-start(bf16[32,4096]{1,0:T(8,128)(2,1)S(1)} %maximum_select_fusion.6), channel_id=1, source_target_pairs={{0,2},{2,0},{4,6},{6,4},{8,10},{10,8},{12,14},{14,12},{1,3},{3,1},... | collective-permute-start | bytes 786440 | tf_op jit(solution)/shard_map/ppermute | solution.py:187
  179.1 18.8 %collective-permute-start.11 = (bf16[64,4096]{1,0:T(8,128)(2,1)S(1)}, bf16[64,4096]{1,0:T(8,128)(2,1)}, u32[]{:S(2)}, u32[]{:S(2)}) collective-permute-start(bf16[64,4096]{1,0:T(8,128)(2,1)S(1)} %maximum_select_fusion.4), channel_id=1, source_target_pairs={{0,1},{1,0},{2,3},{3,2},{4,5},{5,4},{6,7},{7,6},{8,9},{9,8},{10,11... | collective-permute-start | bytes 1572872 | tf_op jit(solution)/shard_map/ppermute | solution.py:191
  191.0 225.5 %all-to-all-start.1 = ((bf16[16,96,4096]{2,1,0:T(8,128)(2,1)}), bf16[16,96,4096]{2,1,0:T(8,128)(2,1)}, u32[]{:S(2)}, u32[]{:S(2)}) async-start(bf16[16,96,4096]{2,1,0:T(8,128)(2,1)} %stack.2), calls=%async_computation.1 | async-start | bytes 25165824 | tf_op jit(solution)/shard_map/all_to_all | solution.py:89
  424.0 27.1 %all-to-all-start.3 = ((bf16[16,8,768]{2,1,0:T(8,128)(2,1)}), bf16[16,8,768]{2,1,0:T(8,128)(2,1)S(1)}, u32[]{:S(2)}, u32[]{:S(2)}) async-start(bf16[16,8,768]{2,1,0:T(8,128)(2,1)} %bitcast.52), calls=%async_computation.3 | async-start | bytes 393216 | tf_op jit(solution)/shard_map/all_to_all | solution.py:223
  (2 other events, 13.7 us)
